TPU v7x, 512 devices: a whole 4x8x8 slice. The times are simulated.
512 devices in a mesh: section: 2 (over core), req: 64 (over y, z), head: 4 (over x).
Axes of the slice: x: 4, y: 8, z: 8, core: 2. Of those that a mesh axis runs over, the one named last changes fastest.
Arguments:
- embedding_per_slot: bfloat16 [512, 4, 1024], P('req', None, 'head'), may hold values from -6 to 6
- tally_per_slot: int32 [512], P('req'), may hold values from 1 to 4
- slot_requests: int32 [512], replicated, may hold values from 0 to 511, as said below
- memory_per_request: float32 [2, 512, 16, 64, 64], P('section', 'req', 'head'), may hold values from -4 to 4
- previous_step_feature: bfloat16 [2, 512, 1024], P('section', 'req', 'head'), may hold values from -6 to 6
- lag_interpolants: bfloat16 [2, 5, 1024], P('section'), may hold values from 0 to 1
- acceptor_projection: bfloat16 [2, 1024, 1024], P('section', None, 'head'), may hold values from -0.1875 to 0.1875
- address_projection: bfloat16 [2, 1024, 1024], P('section', None, 'head'), may hold values from -0.1875 to 0.1875
- content_projection: bfloat16 [2, 1024, 1024], P('section', None, 'head'), may hold values from -0.1875 to 0.1875
- readout_projection: bfloat16 [2, 1024, 1024], P('section', 'head'), may hold values from -0.1875 to 0.1875
- fading_first_lowrank: bfloat16 [2, 1024, 96], P('section', 'head'), may hold values from -0.1875 to 0.1875
- fading_second_lowrank: bfloat16 [2, 96, 1024], P('section', None, 'head'), may hold values from -0.625 to 0.625
- adapt_first_lowrank: bfloat16 [2, 1024, 96], P('section', 'head'), may hold values from -0.1875 to 0.1875
- adapt_second_lowrank: bfloat16 [2, 96, 1024], P('section', None, 'head'), may hold values from -0.625 to 0.625
- fading_baseline: float32 [2, 1024], P('section', 'head'), may hold values from -4 to 1
- adapt_baseline: float32 [2, 1024], P('section', 'head'), may hold values from -3 to 3
- erasing_address_gains: float32 [2, 1024], P('section', 'head'), may hold values from 0.5 to 1.5
- address_rate_coupling: float32 [2, 1024], P('section', 'head'), may hold values from 0 to 1
- present_extra_gain: float32 [2, 1024], P('section', 'head'), may hold values from -3 to 3
- section_standard_gains: float32 [2, 1024], P('section', 'head'), may hold values from 0.1 to 1.9
- section_standard_shift_terms: float32 [2, 1024], P('section', 'head'), may hold values from -2 to 2
Outputs:
- layer_out: bfloat16 [2, 512, 4, 1024], P('section', 'req', None, 'head')
Inputs may be any that keep to these rules, and one draw needn't show every extreme that they name: `slot_requests`: every request appears once. Of one group's 8 arrival slots at most 1 hold requests stored in any one group, and each group holds exactly 1 from some group.
All inputs are finite; a program needn't handle non-finite values.
Results may differ from a plain program's by a relative error of at most 0.02.
Values may be sent and summed in bfloat16 or wider, within the bound.
No kernel may reach another device: no remote copies, remote signals or barrier semaphores. Data moves between devices by JAX's collectives and lax.ppermute only.
A program may use at most 64 MiB of HBM per device.

v0:
```python
import jax
import jax.numpy as jnp
from jax import lax
from jax.sharding import PartitionSpec as P

highest = lax.Precision.HIGHEST


def from_behind(block, axis, distance):
    devices = range(lax.axis_size(axis))
    route = [(i - distance, i) for i in devices if i - distance in devices]
    return lax.ppermute(block, axis, route)


def sequence_recurrence(
    acceptor_entries,
    address_entries,
    content_entries,
    latent_response,
    adapt_latent,
    starting_memory,
    fading_second_lowrank,
    adapt_second_lowrank,
    fading_baseline,
    adapt_baseline,
    erasing_address_gains,
    address_rate_coupling,
    present_extra_gain,
    section_standard_gains,
    section_standard_shift_terms,
):
    batch_rows = starting_memory.shape[0]
    stored_memory_parts = starting_memory.shape[1]
    subspace_span = starting_memory.shape[2]

    def to_heads(array_in):
        return array_in.reshape(batch_rows, -1, stored_memory_parts, subspace_span)

    log_rate = (
        -jax.nn.softplus(
            -(
                fading_baseline
                + jnp.dot(
                    latent_response, fading_second_lowrank, preferred_element_type=jnp.float32
                )
            )
        )
        - 0.5
    )
    decays = to_heads(jnp.exp(-jnp.exp(log_rate)))
    learning = jax.nn.sigmoid(
        adapt_baseline
        + jnp.dot(adapt_latent, adapt_second_lowrank, preferred_element_type=jnp.float32)
    )
    learn_heads = to_heads(learning)
    scaled = to_heads(address_entries * erasing_address_gains)
    normed = scaled / jnp.sqrt(jnp.sum(scaled * scaled, axis=-1, keepdims=True) + 1e-06)
    erasing_address = to_heads(address_entries * (1.0 + (learning - 1.0) * address_rate_coupling))
    acceptor_parts = to_heads(acceptor_entries)
    content_part_lines = to_heads(content_entries)
    states = starting_memory
    readout = []
    for position in range(acceptor_parts.shape[1]):
        pulled = jnp.einsum("rhij,rhj->rhi", states, normed[:, position], precision=highest)
        states = (
            states * decays[:, position][:, :, None, :]
            - jnp.einsum(
                "rhi,rhj->rhij",
                pulled,
                normed[:, position] * learn_heads[:, position],
                precision=highest,
            )
            + jnp.einsum(
                "rhi,rhj->rhij",
                content_part_lines[:, position],
                erasing_address[:, position],
                precision=highest,
            )
        )
        readout.append(
            jnp.einsum("rhij,rhj->rhi", states, acceptor_parts[:, position], precision=highest)
        )
    read_all = jnp.stack(readout, axis=1)
    center = read_all - jnp.mean(read_all, axis=-1, keepdims=True)
    variance = jnp.mean(center * center, axis=-1, keepdims=True)
    gain_heads = section_standard_gains.reshape(stored_memory_parts, subspace_span)
    bias_heads = section_standard_shift_terms.reshape(stored_memory_parts, subspace_span)
    standardized_parts = center / jnp.sqrt(variance + 0.00064) * gain_heads + bias_heads
    present_extra_term = (
        jnp.sum(
            acceptor_parts
            * erasing_address
            * present_extra_gain.reshape(stored_memory_parts, subspace_span),
            axis=-1,
            keepdims=True,
        )
        * content_part_lines
    )
    return (
        (standardized_parts + present_extra_term)
        .astype(jnp.bfloat16)
        .reshape(-1, stored_memory_parts * subspace_span)
    )


def run_sublevel(lowrank_latent, earlier_entry, starting_memory, params):
    (
        lag_interpolants,
        acceptor_projection,
        address_projection,
        content_projection,
        readout_projection,
        fading_first_lowrank,
        fading_second_lowrank,
        adapt_first_lowrank,
        adapt_second_lowrank,
        fading_baseline,
        adapt_baseline,
        erasing_address_gains,
        address_rate_coupling,
        present_extra_gain,
        section_standard_gains,
        section_standard_shift_terms,
    ) = params
    batch_rows, steps_count, shard_width = lowrank_latent.shape
    previous = jnp.concatenate([earlier_entry[:, None, :], lowrank_latent[:, :-1, :]], axis=1)
    piece_now = lax.all_gather(lowrank_latent, "head", axis=2, tiled=True)
    piece_prev = lax.all_gather(previous, "head", axis=2, tiled=True)
    span_width = piece_now.shape[2]
    coef_rows = lag_interpolants.astype(jnp.float32)
    current_piece = piece_now.astype(jnp.float32)
    spread_piece = piece_prev.astype(jnp.float32) - current_piece
    updated = []
    for slot_num, which_mix, weight_all in (
        (0, 0, acceptor_projection),
        (1, 2, address_projection),
        (2, 3, content_projection),
    ):
        blend = (
            (current_piece + spread_piece * coef_rows[which_mix])
            .astype(jnp.bfloat16)
            .reshape(-1, span_width)
        )
        updated.append(jnp.dot(blend, weight_all, preferred_element_type=jnp.float32))
    acceptor_entries = updated[0]
    address_entries = updated[1]
    content_entries = updated[2]
    current = lowrank_latent.astype(jnp.float32)
    spread = previous.astype(jnp.float32) - current
    column_start = lax.axis_index("head") * shard_width
    decay_mix = lax.dynamic_slice_in_dim(lag_interpolants[1], column_start, shard_width, 0).astype(
        jnp.float32
    )
    learn_mix = lax.dynamic_slice_in_dim(lag_interpolants[4], column_start, shard_width, 0).astype(
        jnp.float32
    )
    decay_input = (current + spread * decay_mix).astype(jnp.bfloat16).reshape(-1, shard_width)
    learn_input = (current + spread * learn_mix).astype(jnp.bfloat16).reshape(-1, shard_width)
    partial_rank = jnp.dot(decay_input, fading_first_lowrank, preferred_element_type=jnp.float32)
    partial_learn = jnp.dot(learn_input, adapt_first_lowrank, preferred_element_type=jnp.float32)
    decay_total, learn_total = lax.psum((partial_rank, partial_learn), "head")
    latent_response = jnp.tanh(decay_total).astype(jnp.bfloat16)
    adapt_latent = learn_total.astype(jnp.bfloat16)
    lagged_features = sequence_recurrence(
        acceptor_entries,
        address_entries,
        content_entries,
        latent_response,
        adapt_latent,
        starting_memory,
        fading_second_lowrank,
        adapt_second_lowrank,
        fading_baseline,
        adapt_baseline,
        erasing_address_gains,
        address_rate_coupling,
        present_extra_gain,
        section_standard_gains,
        section_standard_shift_terms,
    )
    own_rows = lax.psum_scatter(
        lax.dot_general(
            readout_projection,
            lagged_features,
            (((0,), (1,)), ((), ())),
            preferred_element_type=jnp.float32,
        ),
        "head",
        scatter_dimension=0,
        tiled=True,
    )
    projected = own_rows.T.reshape(batch_rows, steps_count, shard_width)
    return (current + projected).astype(jnp.bfloat16)


def run_sections(inputs, states_use, last_use, params):
    section_num = lax.axis_index("section")
    section_count = lax.axis_size("section")
    block_count = 1
    block_rows = inputs.shape[0] // block_count
    result = jnp.zeros_like(inputs)
    incoming = jnp.zeros((block_rows,) + inputs.shape[1:], jnp.bfloat16)
    tick_total = block_count + section_count - 1
    for tick_num in range(tick_total):
        lag = tick_num - section_num
        entering = jnp.where(section_num == 0, inputs, incoming)
        produced = run_sublevel(entering, last_use, states_use, params)
        is_valid = (lag >= 0) & (lag < block_count)
        result = jnp.where(is_valid, produced, result)
        if tick_num + 1 < tick_total:
            incoming = from_behind(produced, "section", 1)
    return result


def body(
    embedding_per_slot,
    tally_per_slot,
    slot_requests,
    memory_per_request,
    previous_step_feature,
    lag_interpolants,
    acceptor_projection,
    address_projection,
    content_projection,
    readout_projection,
    fading_first_lowrank,
    fading_second_lowrank,
    adapt_first_lowrank,
    adapt_second_lowrank,
    fading_baseline,
    adapt_baseline,
    erasing_address_gains,
    address_rate_coupling,
    present_extra_gain,
    section_standard_gains,
    section_standard_shift_terms,
):
    local_rows = embedding_per_slot.shape[0]
    groups = lax.axis_size("req")
    capacity = (local_rows + groups - 1) // groups
    my_group = lax.axis_index("req")
    slot_ids = jnp.arange(local_rows, dtype=jnp.int32)
    table = slot_requests.reshape(groups, local_rows)
    my_arrivals = lax.dynamic_index_in_dim(table, my_group, 0, keepdims=False)
    home_group = my_arrivals // local_rows
    earlier = slot_ids[None, :] < slot_ids[:, None]
    arrival_rank = jnp.sum(
        ((home_group[:, None] == home_group[None, :]) & earlier).astype(jnp.int32), axis=1
    )
    arrival_slot = home_group * capacity + arrival_rank
    requests = my_group * local_rows + slot_ids
    total_rows = slot_requests.shape[0]
    found = slot_requests[None, :] == requests[:, None]
    positions = jnp.sum(
        jnp.where(found, jnp.arange(total_rows, dtype=jnp.int32)[None, :], 0), axis=1
    )
    source = positions // local_rows
    within = positions % local_rows
    source_homes = jnp.take(table, source, axis=0) // local_rows
    home_rank = jnp.sum(
        ((source_homes == my_group) & (slot_ids[None, :] < within[:, None])).astype(jnp.int32),
        axis=1,
    )
    home_slot = source * capacity + home_rank
    buffer_rows = groups * capacity
    params = (
        lag_interpolants[0],
        acceptor_projection[0],
        address_projection[0],
        content_projection[0],
        readout_projection[0],
        fading_first_lowrank[0],
        fading_second_lowrank[0],
        adapt_first_lowrank[0],
        adapt_second_lowrank[0],
        fading_baseline[0],
        adapt_baseline[0],
        erasing_address_gains[0],
        address_rate_coupling[0],
        present_extra_gain[0],
        section_standard_gains[0],
        section_standard_shift_terms[0],
    )
    states_local = memory_per_request[0]
    last_local = previous_step_feature[0]
    outgoing = (
        jnp.zeros((buffer_rows,) + embedding_per_slot.shape[1:], jnp.bfloat16)
        .at[arrival_slot]
        .set(embedding_per_slot)
    )
    arrived = lax.all_to_all(outgoing, "req", split_axis=0, concat_axis=0, tiled=True)
    inputs = jnp.take(arrived, home_slot, axis=0)
    result = run_sections(inputs, states_local, last_local, params)
    going_back = (
        jnp.zeros((buffer_rows,) + result.shape[1:], jnp.bfloat16).at[home_slot].set(result)
    )
    returned = lax.all_to_all(going_back, "req", split_axis=0, concat_axis=0, tiled=True)
    result = jnp.take(returned, arrival_slot, axis=0)
    live_mask = (
        jnp.arange(embedding_per_slot.shape[1], dtype=jnp.int32)[None, :] < tally_per_slot[:, None]
    )
    return jnp.where(live_mask[:, :, None], result, jnp.zeros_like(result))[None]


def solution(mesh):
    return jax.shard_map(
        body,
        mesh=mesh,
        in_specs=(
            P("req", None, "head"),
            P("req"),
            P(),
            P("section", "req", "head", None, None),
            P("section", "req", "head"),
            P("section", None, None),
            P("section", None, "head"),
            P("section", None, "head"),
            P("section", None, "head"),
            P("section", "head", None),
            P("section", "head", None),
            P("section", None, "head"),
            P("section", "head", None),
            P("section", None, "head"),
            P("section", "head"),
            P("section", "head"),
            P("section", "head"),
            P("section", "head"),
            P("section", "head"),
            P("section", "head"),
            P("section", "head"),
        ),
        out_specs=P("section", "req", None, "head"),
        check_vma=False,
    )
```

profile of v0, /device:TPU:8, one launch (start us, length us, event | category | flops | bytes accessed | tf_op | source)
XLA Modules:
  0.0 273.9 jit_solution(2103046319629629872)
XLA Ops:
  8.4 2.0 scatter_fusion
  10.3 16.6 %all-to-all-start = ((bf16[64,4,256]{2,1,0:T(4,128)(2,1)}), bf16[64,4,256]{2,1,0:T(4,128)(2,1)S(1)}, u32[]{:S(2)}, u32[]{:S(2)}) async-start(bf16[64,4,256]{2,1,0:T(4,128)(2,1)} %scatter_fusion), calls=%async_computation | async-start | bytes 262144 | tf_op jit(solution)/shard_map/all_to_all | solution.py:291
  36.4 2.2 all-to-all-done
  39.2 12.3 %all_gather.12 = bf16[8,4,1024]{2,0,1:T(8,128)(2,1)S(1)} all-gather(bf16[8,4,256]{2,0,1:T(8,128)(2,1)S(1)} %broadcast_select_fusion.1), channel_id=1, replica_groups=mesh['section'=2,'req'=64,'head'=4] {'head'}, dimensions={2}, use_global_device_ids=true | all-gather | bytes 81920 | tf_op jit(solution)/shard_map/all_gather | solution.py:127
  51.5 11.9 %all_gather.13 = bf16[8,4,1024]{2,0,1:T(8,128)(2,1)S(1)} all-gather(bf16[8,4,256]{2,0,1:T(8,128)(2,1)S(1)} %pad_maximum_fusion.3), channel_id=1, replica_groups=mesh['section'=2,'req'=64,'head'=4] {'head'}, dimensions={2}, use_global_device_ids=true | all-gather | bytes 81920 | tf_op jit(solution)/shard_map/all_gather | solution.py:128
  65.4 16.7 %all-reduce.1 = (bf16[32,96]{1,0:T(8,128)(2,1)S(1)}, f32[32,96]{1,0:T(8,128)S(1)}) all-reduce(f32[32,96]{1,0:T(8,128)S(1)} %fusion.86, f32[32,96]{1,0:T(8,128)S(1)} %fusion.92), channel_id=1, replica_groups=mesh['section'=2,'req'=64,'head'=4] {'head'}, use_global_device_ids=true, to_apply=%region_6.8 | all-reduce | flops 6144 | bytes 43008 | tf_op jit(solution)/shard_map/psum | solution.py:161
  92.2 1.7 fusion.20
  93.9 2.1 fusion.137
  96.7 2.1 fusion.160
  99.6 3.2 %fusion.55 = f32[8,4,1,64]{3,2,1,0:T(1,128)S(1)} fusion(f32[8,4,64]{2,1,0:T(4,128)S(1)} %copy-done.15, f32[8,4,64]{2,1,0:T(4,128)S(1)} %copy.164, f32[8,4,64]{2,1,0:T(4,128)S(1)} %copy-done.9, f32[8,4,64]{2,1,0:T(4,128)S(1)} %bitcast.461, f32[8,4,64]{2,1,0:T(4,128)S(1)} %get-tuple-element.50, f32[8,4,64,1]{2,0,1,3:T(8,128)S(1)} %copy-done.31, ...), kind=kOutput, calls=%fused_computation.72 | convolution fusion | flops 2883584 | bytes 622592 | tf_op jit(solution)/shard_map/rhij,rhj->rhi/dot_general | solution.py:81
  103.5 2.8 %fusion.54 = f32[8,4,1,64]{3,2,1,0:T(1,128)S(1)} fusion(f32[8,4,64,1]{2,3,1,0:T(1,128)S(1)} %bitcast.471, f32[8,4,64]{2,1,0:T(4,128)S(1)} %copy-done.15, f32[8,4,64]{2,1,0:T(4,128)S(1)} %copy.164, f32[8,4,64]{2,1,0:T(4,128)S(1)} %copy-done.9, f32[8,4,64]{2,1,0:T(4,128)S(1)} %bitcast.462, f32[8,4,64]{2,1,0:T(4,128)S(1)} %get-tuple-element.50, ...), kind=kOutput, calls=%fused_computation.71 | convolution fusion | flops 2883584 | bytes 622592 | tf_op jit(solution)/shard_map/rhij,rhj->rhi/dot_general | solution.py:64
  107.0 2.0 multiply_add_fusion.2
  109.1 1.7 fusion.134
  111.5 1.7 fusion.168
  114.0 2.1 fusion.32
  118.4 22.9 %reduce-scatter.3.cloned.1.call-done = f32[256,32]{0,1:T(8,128)} async-done(((f32[1024,32]{0,1:T(8,128)}), f32[256,32]{0,1:T(8,128)}) %reduce-scatter.3.cloned.1.call-update) | async-done | bytes 32784 | tf_op jit(solution)/shard_map/reduce_scatter | solution.py:181
  144.3 12.0 %all_gather.14 = bf16[8,4,1024]{2,0,1:T(8,128)(2,1)S(1)} all-gather(bf16[8,4,256]{2,0,1:T(8,128)(2,1)S(1)} %broadcast_select_fusion), channel_id=1, replica_groups=mesh['section'=2,'req'=64,'head'=4] {'head'}, dimensions={2}, use_global_device_ids=true | all-gather | bytes 81920 | tf_op jit(solution)/shard_map/all_gather | solution.py:127
  156.4 11.9 %all_gather.15 = bf16[8,4,1024]{2,0,1:T(8,128)(2,1)S(1)} all-gather(bf16[8,4,256]{2,0,1:T(8,128)(2,1)S(1)} %pad_maximum_fusion.2), channel_id=1, replica_groups=mesh['section'=2,'req'=64,'head'=4] {'head'}, dimensions={2}, use_global_device_ids=true | all-gather | bytes 81920 | tf_op jit(solution)/shard_map/all_gather | solution.py:128
  171.8 15.1 %all-reduce = (bf16[32,96]{1,0:T(8,128)(2,1)S(1)}, f32[32,96]{1,0:T(8,128)S(1)}) all-reduce(f32[32,96]{1,0:T(8,128)S(1)} %fusion.84, f32[32,96]{1,0:T(8,128)S(1)} %fusion.90), channel_id=1, replica_groups=mesh['section'=2,'req'=64,'head'=4] {'head'}, use_global_device_ids=true, to_apply=%region_13.15 | all-reduce | flops 6144 | bytes 43008 | tf_op jit(solution)/shard_map/psum | solution.py:161
  189.1 1.7 fusion.18
  192.1 2.1 fusion.131
  194.1 2.1 fusion.155
  196.2 3.2 %fusion.57 = f32[8,4,1,64]{3,2,1,0:T(1,128)S(1)} fusion(f32[8,4,64]{2,1,0:T(4,128)S(1)} %get-tuple-element.42, f32[8,4,64]{2,1,0:T(4,128)S(1)} %copy.178, f32[8,4,64]{2,1,0:T(4,128)S(1)} %get-tuple-element.18, f32[8,4,64]{2,1,0:T(4,128)S(1)} %bitcast.464, f32[8,4,64]{2,1,0:T(4,128)S(1)} %get-tuple-element.30, f32[8,4,64,1]{2,0,1,3:T(8,128)S(1)} %get-tuple-element.27, ...), kind=kOutput, calls=%fused_computation.74 | convolution fusion | flops 2883584 | bytes 622592 | tf_op jit(solution)/shard_map/rhij,rhj->rhi/dot_general | solution.py:81
  199.5 2.8 %fusion.56 = f32[8,4,1,64]{3,2,1,0:T(1,128)S(1)} fusion(f32[8,4,64,1]{2,3,1,0:T(1,128)S(1)} %bitcast.473, f32[8,4,64]{2,1,0:T(4,128)S(1)} %get-tuple-element.42, f32[8,4,64]{2,1,0:T(4,128)S(1)} %copy.178, f32[8,4,64]{2,1,0:T(4,128)S(1)} %get-tuple-element.18, f32[8,4,64]{2,1,0:T(4,128)S(1)} %bitcast.465, f32[8,4,64]{2,1,0:T(4,128)S(1)} %get-tuple-element.30, ...), kind=kOutput, calls=%fused_computation.73 | convolution fusion | flops 2883584 | bytes 622592 | tf_op jit(solution)/shard_map/rhij,rhj->rhi/dot_general | solution.py:64
  202.3 2.0 multiply_add_fusion
  204.3 1.7 fusion.128
  206.1 1.7 fusion.169
  207.8 2.1 fusion.26
  213.6 23.6 %reduce-scatter.5.cloned.1.call-done = f32[256,32]{0,1:T(8,128)} async-done(((f32[1024,32]{0,1:T(8,128)}), f32[256,32]{0,1:T(8,128)}) %reduce-scatter.5.cloned.1.call-update) | async-done | bytes 32784 | tf_op jit(solution)/shard_map/reduce_scatter | solution.py:181
  238.7 1.9 scatter_fusion.1
  240.6 13.4 %all-to-all-start.1 = ((bf16[64,4,256]{2,1,0:T(4,128)(2,1)}), bf16[64,4,256]{2,1,0:T(4,128)(2,1)S(1)}, u32[]{:S(2)}, u32[]{:S(2)}) async-start(bf16[64,4,256]{2,1,0:T(4,128)(2,1)} %scatter_fusion.1), calls=%async_computation.3 | async-start | bytes 262144 | tf_op jit(solution)/shard_map/all_to_all | solution.py:297
  254.7 11.1 %all-to-all-done.1 = bf16[64,4,256]{2,1,0:T(4,128)(2,1)S(1)} async-done(((bf16[64,4,256]{2,1,0:T(4,128)(2,1)}), bf16[64,4,256]{2,1,0:T(4,128)(2,1)S(1)}, u32[]{:S(2)}, u32[]{:S(2)}) %all-to-all-start.1) | async-done | bytes 131104 | tf_op jit(solution)/shard_map/all_to_all | solution.py:297
  (268 shorter events, 47.0 us)
Async XLA Ops:
  6.5 111.0 %copy-start = (bf16[1,256,1024]{2,1,0:T(8,128)(2,1)S(1)}, bf16[1,256,1024]{2,1,0:T(8,128)(2,1)}, u32[]{:S(2)}) copy-start(bf16[1,256,1024]{2,1,0:T(8,128)(2,1)} %param.32) | copy-start | bytes 1572868
  6.5 23.3 %copy-start.3 = (bf16[1,1024,256]{2,1,0:T(8,128)(2,1)S(1)}, bf16[1,1024,256]{2,1,0:T(8,128)(2,1)}, u32[]{:S(2)}) copy-start(bf16[1,1024,256]{2,1,0:T(8,128)(2,1)} %param.29) | copy-start | bytes 1572868
  7.4 20.9 %copy-start.8 = (s32[64,8]{1,0:T(8,128)}, s32[64,8]{1,0:T(8,128)S(1)}, u32[]{:S(2)}) copy-start(s32[64,8]{1,0:T(8,128)S(1)} %reshape.364) | copy-start | bytes 6148
  10.3 28.2 %all-to-all-start = ((bf16[64,4,256]{2,1,0:T(4,128)(2,1)}), bf16[64,4,256]{2,1,0:T(4,128)(2,1)S(1)}, u32[]{:S(2)}, u32[]{:S(2)}) async-start(bf16[64,4,256]{2,1,0:T(4,128)(2,1)} %scatter_fusion), calls=%async_computation | async-start | bytes 262144 | tf_op jit(solution)/shard_map/all_to_all | solution.py:291
  26.9 114.4 %reduce-scatter.3.cloned.1.call-start = ((), (), s32[]{:S(2)}) async-start(), calls=%async_computation.4 | async-start | bytes 163840 | tf_op jit(solution)/shard_map/reduce_scatter | solution.py:181
  28.9 0.8 copy-start.25
  29.7 33.8 %copy-start.33 = (pred[8]{0:T(512)(128)(4,1)}, pred[8]{0:T(512)(128)(4,1)S(1)}, u32[]{:S(2)}) copy-start(pred[8]{0:T(512)(128)(4,1)S(1)} %get-tuple-element.12) | copy-start | bytes 28
  29.8 33.8 %copy-start.35 = (f32[1,1,256]{2,1,0:T(1,128)}, f32[1,1,256]{2,1,0:T(1,128)S(1)}, u32[]{:S(2)}) copy-start(f32[1,1,256]{2,1,0:T(1,128)S(1)} %get-tuple-element.77) | copy-start | bytes 3076
  29.8 33.8 %copy-start.37 = (f32[1,1,256]{2,1,0:T(1,128)}, f32[1,1,256]{2,1,0:T(1,128)S(1)}, u32[]{:S(2)}) copy-start(f32[1,1,256]{2,1,0:T(1,128)S(1)} %get-tuple-element.78) | copy-start | bytes 3076
  29.8 1.0 copy-start.4
  36.4 27.0 %copy-start.23 = (f32[1,1,1024]{2,1,0:T(1,128)}, f32[1,1,1024]{2,1,0:T(1,128)S(1)}, u32[]{:S(2)}) copy-start(f32[1,1,1024]{2,1,0:T(1,128)S(1)} %get-tuple-element.73) | copy-start | bytes 12292
  36.4 49.2 %copy-start.21 = (f32[1,1,1024]{2,1,0:T(1,128)}, f32[1,1,1024]{2,1,0:T(1,128)S(1)}, u32[]{:S(2)}) copy-start(f32[1,1,1024]{2,1,0:T(1,128)S(1)} %get-tuple-element.72) | copy-start | bytes 12292
  39.2 12.3 %copy-start.17 = (bf16[1,8,256]{2,1,0:T(8,128)(2,1)S(1)}, bf16[1,8,256]{2,1,0:T(8,128)(2,1)}, u32[]{:S(2)}) copy-start(bf16[1,8,256]{2,1,0:T(8,128)(2,1)} %param.27) | copy-start | bytes 12292
  63.4 19.7 %copy-start.2 = (bf16[1,1024,256]{2,1,0:T(8,128)(2,1)S(1)}, bf16[1,1024,256]{2,1,0:T(8,128)(2,1)}, u32[]{:S(2)}) copy-start(bf16[1,1024,256]{2,1,0:T(8,128)(2,1)} %param.30) | copy-start | bytes 1572868
  63.6 0.8 copy-start.5
  64.5 0.8 copy-start.6
  65.2 16.9 %copy-start.55 = (bf16[1,96,256]{2,1,0:T(8,128)(2,1)S(1)}, bf16[1,96,256]{2,1,0:T(8,128)(2,1)}, u32[]{:S(2)}) copy-start(bf16[1,96,256]{2,1,0:T(8,128)(2,1)} %param.36) | copy-start | bytes 147460
  85.6 5.9 %copy-start.1 = (f32[1,8,4,64,64]{4,3,2,1,0:T(8,128)S(1)}, f32[1,8,4,64,64]{4,3,2,1,0:T(8,128)}, u32[]{:S(2)}) copy-start(f32[1,8,4,64,64]{4,3,2,1,0:T(8,128)} %param.26) | copy-start | bytes 1572868
  92.2 1.7 copy-start.10
  92.2 1.7 copy-start.16
  92.2 1.8 copy-start.32
  96.7 2.1 copy-start.31
  107.0 2.0 copy-start.12
  111.5 1.8 copy-start.28
  118.4 118.8 %reduce-scatter.5.cloned.1.call-start = ((), (), s32[]{:S(2)}) async-start(), calls=%async_computation.5 | async-start | bytes 163840 | tf_op jit(solution)/shard_map/reduce_scatter | solution.py:181
  142.1 2.1 collective-permute-start
  144.3 12.0 %copy-start.18 = (bf16[1,8,256]{2,1,0:T(8,128)(2,1)S(1)}, bf16[1,8,256]{2,1,0:T(8,128)(2,1)}, u32[]{:S(2)}) copy-start(bf16[1,8,256]{2,1,0:T(8,128)(2,1)} %param.27) | copy-start | bytes 12292
  156.4 11.9 %copy-start.22 = (f32[1,1,1024]{2,1,0:T(1,128)S(1)}, f32[1,1,1024]{2,1,0:T(1,128)}, u32[]{:S(2)}) copy-start(f32[1,1,1024]{2,1,0:T(1,128)} %copy-done.21) | copy-start | bytes 12292
  170.9 0.8 copy-start.7
  171.7 15.3 %copy-start.56 = (bf16[1,96,256]{2,1,0:T(8,128)(2,1)S(1)}, bf16[1,96,256]{2,1,0:T(8,128)(2,1)}, u32[]{:S(2)}) copy-start(bf16[1,96,256]{2,1,0:T(8,128)(2,1)} %param.36) | copy-start | bytes 147460
  190.9 0.8 copy-start.57
  240.6 25.1 %all-to-all-start.1 = ((bf16[64,4,256]{2,1,0:T(4,128)(2,1)}), bf16[64,4,256]{2,1,0:T(4,128)(2,1)S(1)}, u32[]{:S(2)}, u32[]{:S(2)}) async-start(bf16[64,4,256]{2,1,0:T(4,128)(2,1)} %scatter_fusion.1), calls=%async_computation.3 | async-start | bytes 262144 | tf_op jit(solution)/shard_map/all_to_all | solution.py:297
  (36 other events, 24.8 us)
Sparse Core Ops, SparseCore 0:
  118.5 22.7 reduce-scatter.2
  211.7 25.4 reduce-scatter.4
where the time goes:
time: 276 us; the launch traced here: 274 us
  blocking collectives  80 us (29%)
  waiting for transfers between devices  60.6 us (22%)
  matrix products  40.9 us (15%)
  local copies, waits for them, and re-layouts  35.8 us (13%)
  starting transfers between devices  31.3 us (11%)
  between operations  14.4 us (5%)
  other arithmetic  11 us (4%)
    reduce_scatter x2, waiting for transfers between devices, run_sublevel(): lax.psum_scatter(lax.dot_general(readout_projection, lagged_features, (((...  46.5 us
    psum x2, blocking collectives, run_sublevel(): decay_total, learn_total = lax.psum((partial_rank, partial_learn), 'head')  31.9 us
    all_gather x2, blocking collectives, run_sublevel(): piece_now = lax.all_gather(lowrank_latent, 'head', axis=2, tiled=True)  24.4 us
    all_gather x2, blocking collectives, run_sublevel(): piece_prev = lax.all_gather(previous, 'head', axis=2, tiled=True)  23.7 us
    unnamed x129, local copies, waits for them, and re-layouts  19.1 us
    dot_general x8, matrix products, sequence_recurrence(): jnp.einsum('rhij,rhj->rhi', states, acceptor_parts[:, position], precisio...  18.2 us
    dot_general x8, matrix products, sequence_recurrence(): jnp.einsum('rhij,rhj->rhi', states, normed[:, position], precision=highest)  16.7 us
    all_to_all x1, starting transfers between devices, body(): lax.all_to_all(outgoing, 'req', split_axis=0, concat_axis=0, tiled=True)  16.6 us
  transfers between devices with their start and end apart: 5, of which 5 were waited for; matrix products, arithmetic and copies ran while one was open for 3% of the time, Pallas kernels for 0%

commit v1 on v0

--- a/solution.py
+++ b/solution.py
@@ -125,7 +125,12 @@
     batch_rows, steps_count, shard_width = lowrank_latent.shape
     previous = jnp.concatenate([earlier_entry[:, None, :], lowrank_latent[:, :-1, :]], axis=1)
     piece_now = lax.all_gather(lowrank_latent, "head", axis=2, tiled=True)
-    piece_prev = lax.all_gather(previous, "head", axis=2, tiled=True)
+    piece_prev = jnp.concatenate(
+        lax.all_to_all(
+            jnp.stack(tuple((previous for _ in range(lax.psum(1, "head"))))), "head", 0, 0
+        ),
+        axis=2,
+    )
     span_width = piece_now.shape[2]
     coef_rows = lag_interpolants.astype(jnp.float32)
     current_piece = piece_now.astype(jnp.float32)

time: 276 us -> 266 us (0.964)
  blocking collectives: 80 us -> 58.9 us
  starting transfers between devices: 31.3 us -> 39.1 us
  local copies, waits for them, and re-layouts: 35.8 us -> 40.3 us
    all_gather x2 -> x0, blocking collectives: 23.7 us -> none  [run_sublevel(): piece_prev = lax.all_gather(previous, 'head', axis=2, tiled=True)]
    all_to_all x0 -> x2, starting transfers between devices: none -> 7.8 us  [run_sublevel(): lax.all_to_all(jnp.stack(tuple((previous for _ in range(lax.psum(1, 'head...]
    unnamed x129 -> x131, local copies, waits for them, and re-layouts: 19.1 us -> 22.3 us
    psum x2, blocking collectives: 31.9 us -> 34.8 us  [run_sublevel(): decay_total, learn_total = lax.psum((partial_rank, partial_learn), 'head')]
  transfers between devices with their start and end apart: 5 -> 7, of which waited for: 5 -> 5; matrix products, arithmetic and copies ran while one was open for 3% -> 4% of each run, Pallas kernels for 0% -> 0%
where the time goes in v1:
time: 266 us; the launch traced here: 264 us
  waiting for transfers between devices  60.6 us (23%)
  blocking collectives  58.9 us (22%)
  local copies, waits for them, and re-layouts  40.3 us (15%)
  matrix products  40 us (15%)
  starting transfers between devices  39.1 us (15%)
  between operations  14.4 us (5%)
  other arithmetic  10.9 us (4%)
    reduce_scatter x2, waiting for transfers between devices, run_sublevel(): lax.psum_scatter(lax.dot_general(readout_projection, lagged_features, (((...  46.5 us
    psum x2, blocking collectives, run_sublevel(): decay_total, learn_total = lax.psum((partial_rank, partial_learn), 'head')  34.8 us
    all_gather x2, blocking collectives, run_sublevel(): piece_now = lax.all_gather(lowrank_latent, 'head', axis=2, tiled=True)  24.1 us
    unnamed x131, local copies, waits for them, and re-layouts  22.3 us
    dot_general x8, matrix products, sequence_recurrence(): jnp.einsum('rhij,rhj->rhi', states, acceptor_parts[:, position], precisio...  18.2 us
    dot_general x8, matrix products, sequence_recurrence(): jnp.einsum('rhij,rhj->rhi', states, normed[:, position], precision=highest)  16.7 us
    all_to_all x1, starting transfers between devices, body(): lax.all_to_all(outgoing, 'req', split_axis=0, concat_axis=0, tiled=True)  16.6 us
    all_to_all x1, starting transfers between devices, body(): lax.all_to_all(going_back, 'req', split_axis=0, concat_axis=0, tiled=True)  13.4 us
  transfers between devices with their start and end apart: 7, of which 5 were waited for; matrix products, arithmetic and copies ran while one was open for 4% of the time, Pallas kernels for 0%

profile of v1, /device:TPU:8, one launch (start us, length us, event | category | flops | bytes accessed | tf_op | source)
XLA Modules:
  0.0 264.3 jit_solution(10844532490726261195)
XLA Ops:
  8.9 2.0 scatter_fusion
  10.9 16.6 %all-to-all-start = ((bf16[64,4,256]{2,1,0:T(4,128)(2,1)}), bf16[64,4,256]{2,1,0:T(4,128)(2,1)S(1)}, u32[]{:S(2)}, u32[]{:S(2)}) async-start(bf16[64,4,256]{2,1,0:T(4,128)(2,1)} %scatter_fusion), calls=%async_computation | async-start | bytes 262144 | tf_op jit(solution)/shard_map/all_to_all | solution.py:296
  36.9 2.2 all-to-all-done
  41.0 4.3 %all-to-all-start.1 = ((bf16[4,8,4,256]{3,2,1,0:T(4,128)(2,1)}), bf16[4,8,4,256]{3,2,1,0:T(4,128)(2,1)S(1)}, u32[]{:S(2)}, u32[]{:S(2)}) async-start(bf16[4,8,4,256]{3,2,1,0:T(4,128)(2,1)} %stack.44), calls=%async_computation.1 | async-start | bytes 131072 | tf_op jit(solution)/shard_map/all_to_all | solution.py:129
  47.1 17.6 %all-reduce.1 = (bf16[32,96]{1,0:T(8,128)(2,1)S(1)}, f32[32,96]{1,0:T(8,128)S(1)}) all-reduce(f32[32,96]{1,0:T(8,128)S(1)} %fusion.86, f32[32,96]{1,0:T(8,128)S(1)} %fusion.92), channel_id=1, replica_groups=mesh['section'=2,'req'=64,'head'=4] {'head'}, use_global_device_ids=true, to_apply=%region_6.8 | all-reduce | flops 6144 | bytes 43008 | tf_op jit(solution)/shard_map/psum | solution.py:166
  67.3 12.2 %all_gather.6 = bf16[8,4,1024]{2,0,1:T(8,128)(2,1)S(1)} all-gather(bf16[8,4,256]{2,0,1:T(8,128)(2,1)S(1)} %broadcast_select_fusion.1), channel_id=1, replica_groups=mesh['section'=2,'req'=64,'head'=4] {'head'}, dimensions={2}, use_global_device_ids=true | all-gather | bytes 81920 | tf_op jit(solution)/shard_map/all_gather | solution.py:127
  87.1 1.7 fusion.20
  88.8 2.1 fusion.137
  91.6 2.1 fusion.160
  94.4 3.2 %fusion.55 = f32[8,4,1,64]{3,2,1,0:T(1,128)S(1)} fusion(f32[8,4,64]{2,1,0:T(4,128)S(1)} %get-tuple-element.62, f32[8,4,64]{2,1,0:T(4,128)S(1)} %copy.174, f32[8,4,64]{2,1,0:T(4,128)S(1)} %copy-done.9, f32[8,4,64]{2,1,0:T(4,128)S(1)} %bitcast.473, f32[8,4,64]{2,1,0:T(4,128)S(1)} %copy-done.12, f32[8,4,64,1]{2,0,1,3:T(8,128)S(1)} %copy-done.31, ...), kind=kOutput, calls=%fused_computation.72 | convolution fusion | flops 2883584 | bytes 622592 | tf_op jit(solution)/shard_map/rhij,rhj->rhi/dot_general | solution.py:81
  98.4 2.8 %fusion.54 = f32[8,4,1,64]{3,2,1,0:T(1,128)S(1)} fusion(f32[8,4,64,1]{2,3,1,0:T(1,128)S(1)} %bitcast.483, f32[8,4,64]{2,1,0:T(4,128)S(1)} %get-tuple-element.62, f32[8,4,64]{2,1,0:T(4,128)S(1)} %copy.174, f32[8,4,64]{2,1,0:T(4,128)S(1)} %copy-done.9, f32[8,4,64]{2,1,0:T(4,128)S(1)} %bitcast.474, f32[8,4,64]{2,1,0:T(4,128)S(1)} %copy-done.12, ...), kind=kOutput, calls=%fused_computation.71 | convolution fusion | flops 2883584 | bytes 622592 | tf_op jit(solution)/shard_map/rhij,rhj->rhi/dot_general | solution.py:64
  101.9 2.0 multiply_add_fusion.2
  103.9 1.7 fusion.134
  106.4 1.7 fusion.168
  108.9 2.1 fusion.32
  113.3 22.8 %reduce-scatter.3.cloned.1.call-done = f32[256,32]{0,1:T(8,128)} async-done(((f32[1024,32]{0,1:T(8,128)}), f32[256,32]{0,1:T(8,128)}) %reduce-scatter.3.cloned.1.call-update) | async-done | bytes 32784 | tf_op jit(solution)/shard_map/reduce_scatter | solution.py:186
  141.1 3.5 %all-to-all-start.2 = ((bf16[4,8,4,256]{3,2,1,0:T(4,128)(2,1)}), bf16[4,8,4,256]{3,2,1,0:T(4,128)(2,1)S(1)}, u32[]{:S(2)}, u32[]{:S(2)}) async-start(bf16[4,8,4,256]{3,2,1,0:T(4,128)(2,1)} %stack.50), calls=%async_computation.3 | async-start | bytes 131072 | tf_op jit(solution)/shard_map/all_to_all | solution.py:129
  145.8 17.3 %all-reduce = (bf16[32,96]{1,0:T(8,128)(2,1)S(1)}, f32[32,96]{1,0:T(8,128)S(1)}) all-reduce(f32[32,96]{1,0:T(8,128)S(1)} %fusion.84, f32[32,96]{1,0:T(8,128)S(1)} %fusion.90), channel_id=1, replica_groups=mesh['section'=2,'req'=64,'head'=4] {'head'}, use_global_device_ids=true, to_apply=%region_13.15 | all-reduce | flops 6144 | bytes 43008 | tf_op jit(solution)/shard_map/psum | solution.py:166
  165.0 11.9 %all_gather.7 = bf16[8,4,1024]{2,0,1:T(8,128)(2,1)S(1)} all-gather(bf16[8,4,256]{2,0,1:T(8,128)(2,1)S(1)} %broadcast_select_fusion), channel_id=1, replica_groups=mesh['section'=2,'req'=64,'head'=4] {'head'}, dimensions={2}, use_global_device_ids=true | all-gather | bytes 81920 | tf_op jit(solution)/shard_map/all_gather | solution.py:127
  180.6 1.7 fusion.18
  182.5 2.1 fusion.131
  184.6 2.1 fusion.155
  186.7 3.2 %fusion.57 = f32[8,4,1,64]{3,2,1,0:T(1,128)S(1)} fusion(f32[8,4,64]{2,1,0:T(4,128)S(1)} %get-tuple-element.42, f32[8,4,64]{2,1,0:T(4,128)S(1)} %copy.190, f32[8,4,64]{2,1,0:T(4,128)S(1)} %get-tuple-element.18, f32[8,4,64]{2,1,0:T(4,128)S(1)} %bitcast.476, f32[8,4,64]{2,1,0:T(4,128)S(1)} %get-tuple-element.30, f32[8,4,64,1]{2,0,1,3:T(8,128)S(1)} %get-tuple-element.27, ...), kind=kOutput, calls=%fused_computation.74 | convolution fusion | flops 2883584 | bytes 622592 | tf_op jit(solution)/shard_map/rhij,rhj->rhi/dot_general | solution.py:81
  189.9 2.8 %fusion.56 = f32[8,4,1,64]{3,2,1,0:T(1,128)S(1)} fusion(f32[8,4,64,1]{2,3,1,0:T(1,128)S(1)} %bitcast.485, f32[8,4,64]{2,1,0:T(4,128)S(1)} %get-tuple-element.42, f32[8,4,64]{2,1,0:T(4,128)S(1)} %copy.190, f32[8,4,64]{2,1,0:T(4,128)S(1)} %get-tuple-element.18, f32[8,4,64]{2,1,0:T(4,128)S(1)} %bitcast.477, f32[8,4,64]{2,1,0:T(4,128)S(1)} %get-tuple-element.30, ...), kind=kOutput, calls=%fused_computation.73 | convolution fusion | flops 2883584 | bytes 622592 | tf_op jit(solution)/shard_map/rhij,rhj->rhi/dot_general | solution.py:64
  192.8 2.0 multiply_add_fusion
  194.8 1.7 fusion.128
  196.6 1.7 fusion.169
  198.3 2.1 fusion.26
  204.0 23.7 %reduce-scatter.5.cloned.1.call-done = f32[256,32]{0,1:T(8,128)} async-done(((f32[1024,32]{0,1:T(8,128)}), f32[256,32]{0,1:T(8,128)}) %reduce-scatter.5.cloned.1.call-update) | async-done | bytes 32784 | tf_op jit(solution)/shard_map/reduce_scatter | solution.py:186
  229.2 1.9 scatter_fusion.1
  231.1 13.4 %all-to-all-start.3 = ((bf16[64,4,256]{2,1,0:T(4,128)(2,1)}), bf16[64,4,256]{2,1,0:T(4,128)(2,1)S(1)}, u32[]{:S(2)}, u32[]{:S(2)}) async-start(bf16[64,4,256]{2,1,0:T(4,128)(2,1)} %scatter_fusion.1), calls=%async_computation.5 | async-start | bytes 262144 | tf_op jit(solution)/shard_map/all_to_all | solution.py:302
  245.1 11.1 %all-to-all-done.3 = bf16[64,4,256]{2,1,0:T(4,128)(2,1)S(1)} async-done(((bf16[64,4,256]{2,1,0:T(4,128)(2,1)}), bf16[64,4,256]{2,1,0:T(4,128)(2,1)S(1)}, u32[]{:S(2)}, u32[]{:S(2)}) %all-to-all-start.3) | async-done | bytes 131104 | tf_op jit(solution)/shard_map/all_to_all | solution.py:302
  (280 shorter events, 50.6 us)
Async XLA Ops:
  6.5 105.8 %copy-start = (bf16[1,256,1024]{2,1,0:T(8,128)(2,1)S(1)}, bf16[1,256,1024]{2,1,0:T(8,128)(2,1)}, u32[]{:S(2)}) copy-start(bf16[1,256,1024]{2,1,0:T(8,128)(2,1)} %param.32) | copy-start | bytes 1572868
  6.5 23.8 %copy-start.3 = (bf16[1,1024,256]{2,1,0:T(8,128)(2,1)S(1)}, bf16[1,1024,256]{2,1,0:T(8,128)(2,1)}, u32[]{:S(2)}) copy-start(bf16[1,1024,256]{2,1,0:T(8,128)(2,1)} %param.29) | copy-start | bytes 1572868
  7.4 21.5 %copy-start.8 = (s32[64,8]{1,0:T(8,128)}, s32[64,8]{1,0:T(8,128)S(1)}, u32[]{:S(2)}) copy-start(s32[64,8]{1,0:T(8,128)S(1)} %reshape.376) | copy-start | bytes 6148
  10.9 28.2 %all-to-all-start = ((bf16[64,4,256]{2,1,0:T(4,128)(2,1)}), bf16[64,4,256]{2,1,0:T(4,128)(2,1)S(1)}, u32[]{:S(2)}, u32[]{:S(2)}) async-start(bf16[64,4,256]{2,1,0:T(4,128)(2,1)} %scatter_fusion), calls=%async_computation | async-start | bytes 262144 | tf_op jit(solution)/shard_map/all_to_all | solution.py:296
  29.5 0.8 copy-start.25
  30.2 15.1 %copy-start.33 = (pred[8]{0:T(512)(128)(4,1)}, pred[8]{0:T(512)(128)(4,1)S(1)}, u32[]{:S(2)}) copy-start(pred[8]{0:T(512)(128)(4,1)S(1)} %get-tuple-element.12) | copy-start | bytes 28
  30.3 15.0 %copy-start.35 = (f32[1,1,256]{2,1,0:T(1,128)}, f32[1,1,256]{2,1,0:T(1,128)S(1)}, u32[]{:S(2)}) copy-start(f32[1,1,256]{2,1,0:T(1,128)S(1)} %get-tuple-element.77) | copy-start | bytes 3076
  30.3 15.0 %copy-start.37 = (f32[1,1,256]{2,1,0:T(1,128)}, f32[1,1,256]{2,1,0:T(1,128)S(1)}, u32[]{:S(2)}) copy-start(f32[1,1,256]{2,1,0:T(1,128)S(1)} %get-tuple-element.78) | copy-start | bytes 3076
  30.3 1.0 copy-start.4
  36.9 42.6 %copy-start.21 = (f32[1,1,1024]{2,1,0:T(1,128)}, f32[1,1,1024]{2,1,0:T(1,128)S(1)}, u32[]{:S(2)}) copy-start(f32[1,1,1024]{2,1,0:T(1,128)S(1)} %get-tuple-element.73) | copy-start | bytes 12292
  41.0 38.5 %all-to-all-start.1 = ((bf16[4,8,4,256]{3,2,1,0:T(4,128)(2,1)}), bf16[4,8,4,256]{3,2,1,0:T(4,128)(2,1)S(1)}, u32[]{:S(2)}, u32[]{:S(2)}) async-start(bf16[4,8,4,256]{3,2,1,0:T(4,128)(2,1)} %stack.44), calls=%async_computation.1 | async-start | bytes 131072 | tf_op jit(solution)/shard_map/all_to_all | solution.py:129
  45.3 90.8 %reduce-scatter.3.cloned.1.call-start = ((), (), s32[]{:S(2)}) async-start(), calls=%async_computation.6 | async-start | bytes 163840 | tf_op jit(solution)/shard_map/reduce_scatter | solution.py:186
  45.4 0.8 copy-start.5
  46.2 0.8 copy-start.6
  47.0 17.7 %copy-start.57 = (bf16[1,96,256]{2,1,0:T(8,128)(2,1)S(1)}, bf16[1,96,256]{2,1,0:T(8,128)(2,1)}, u32[]{:S(2)}) copy-start(bf16[1,96,256]{2,1,0:T(8,128)(2,1)} %param.34) | copy-start | bytes 147460
  65.6 0.8 copy-start.55
  67.3 12.4 %copy-start.2 = (bf16[1,1024,256]{2,1,0:T(8,128)(2,1)S(1)}, bf16[1,1024,256]{2,1,0:T(8,128)(2,1)}, u32[]{:S(2)}) copy-start(bf16[1,1024,256]{2,1,0:T(8,128)(2,1)} %param.30) | copy-start | bytes 1572868
  83.4 2.9 %copy-start.1 = (f32[1,8,4,64,64]{4,3,2,1,0:T(8,128)S(1)}, f32[1,8,4,64,64]{4,3,2,1,0:T(8,128)}, u32[]{:S(2)}) copy-start(f32[1,8,4,64,64]{4,3,2,1,0:T(8,128)} %param.26) | copy-start | bytes 1572868
  87.0 1.7 copy-start.10
  87.0 1.7 copy-start.13
  87.0 1.8 copy-start.32
  91.6 2.1 copy-start.31
  101.9 2.0 copy-start.15
  106.4 1.8 copy-start.28
  136.1 0.8 copy-start.34
  136.9 2.1 collective-permute-start
  141.1 35.7 %all-to-all-start.2 = ((bf16[4,8,4,256]{3,2,1,0:T(4,128)(2,1)}), bf16[4,8,4,256]{3,2,1,0:T(4,128)(2,1)S(1)}, u32[]{:S(2)}, u32[]{:S(2)}) async-start(bf16[4,8,4,256]{3,2,1,0:T(4,128)(2,1)} %stack.50), calls=%async_computation.3 | async-start | bytes 131072 | tf_op jit(solution)/shard_map/all_to_all | solution.py:129
  144.7 83.0 %reduce-scatter.5.cloned.1.call-start = ((), (), s32[]{:S(2)}) async-start(), calls=%async_computation.7 | async-start | bytes 163840 | tf_op jit(solution)/shard_map/reduce_scatter | solution.py:186
  144.9 0.8 copy-start.7
  145.7 17.4 %copy-start.56 = (bf16[1,96,256]{2,1,0:T(8,128)(2,1)S(1)}, bf16[1,96,256]{2,1,0:T(8,128)(2,1)}, u32[]{:S(2)}) copy-start(bf16[1,96,256]{2,1,0:T(8,128)(2,1)} %param.36) | copy-start | bytes 147460
  163.8 0.8 copy-start.58
  231.1 25.1 %all-to-all-start.3 = ((bf16[64,4,256]{2,1,0:T(4,128)(2,1)}), bf16[64,4,256]{2,1,0:T(4,128)(2,1)S(1)}, u32[]{:S(2)}, u32[]{:S(2)}) async-start(bf16[64,4,256]{2,1,0:T(4,128)(2,1)} %scatter_fusion.1), calls=%async_computation.5 | async-start | bytes 262144 | tf_op jit(solution)/shard_map/all_to_all | solution.py:302
  (39 other events, 26.5 us)
Sparse Core Ops, SparseCore 0:
  113.4 22.6 reduce-scatter.2
  202.1 25.4 reduce-scatter.4
